TPU v7x, 128 devices: a whole 4x4x4 slice. The times are simulated.
128 devices in a mesh: row: 16 (over z_lo, x, core), col: 8 (over y, z_hi).
Axes of the slice: x: 4, y: 4, z: 4 (z_hi: 2, z_lo: 2; z = z_hi * 2 + z_lo), core: 2. Of those that a mesh axis runs over, the one named last changes fastest.
Arguments:
- shared_rows: float32 [2048, 16384], P('row', 'col'), may hold values from -0.125 to 0.125
- event_counts: int32 [16], replicated, may hold values from 32 to 128, as said below
- ridge: float32 [16384], P('col'), may hold values from 0.5 to 2
- items: float32 [1024, 16384], P('row', 'col'), may hold values from -6 to 6
- cand_ids: int32 [512], replicated, may hold values from 0 to 1023
- theta: float32 [16384], P('col'), may hold values from -0.046875 to 0.046875
Outputs:
- gram_tile: float32 [16384, 16384], P('row', 'col')
- scores: float32 [512], replicated
Inputs may be any that keep to these rules, and one draw needn't show every extreme that they name: event_counts[s] counts the live slots at the start of row shard s's 128 slots; some shard is full.
All inputs are finite; a program needn't handle non-finite values.
Results may differ from a plain program's by a relative error of at most 0.000068.
Values sent between devices are 32-bit elements; how exact they have to be, the bound alone decides.
No kernel may reach another device: no remote copies, remote signals or barrier semaphores. Data moves between devices by JAX's collectives and lax.ppermute only.
A program may use at most 128 MiB of HBM per device.

v0:
```python
import jax
import jax.numpy as jnp
from jax import lax
from jax.sharding import PartitionSpec as P

F = 16384
high = lax.Precision.HIGHEST


def spread(value, axis, source):
    kept = jnp.where(lax.axis_index(axis) == source, value, 0).astype(value.dtype)
    return lax.psum(kept, axis)


def body(shared_rows, event_counts, ridge, items, cand_ids, theta):
    ratio = lax.axis_size("row") // lax.axis_size("col")
    row_pos = lax.axis_index("row")
    col_pos = lax.axis_index("col")
    width_col = shared_rows.shape[1]
    width_row = width_col // ratio
    ev_slots = shared_rows.shape[0]
    slot = lax.iota(jnp.int32, ev_slots)
    masked = jnp.where((slot < event_counts[row_pos])[:, None], shared_rows, jnp.float32(0.0))
    offset = row_pos % ratio * width_row
    root = row_pos // ratio
    contract = (((0,), (0,)), ((), ()))
    col_all = lax.all_gather(masked, "row", axis=0, tiled=True)
    row_all = spread(lax.dynamic_slice_in_dim(col_all, offset, width_row, 1), "col", root)
    tile = lax.dot_general(
        row_all, col_all, contract, precision=high, preferred_element_type=jnp.float32
    )
    rows_global = row_pos * width_row + lax.broadcasted_iota(jnp.int32, (width_row, width_col), 0)
    cols_global = col_pos * width_col + lax.broadcasted_iota(jnp.int32, (width_row, width_col), 1)
    tile = tile + jnp.where(rows_global == cols_global, ridge[None, :], jnp.float32(0.0))
    items_dev = items.shape[0]
    onehot = (
        cand_ids[:, None] == row_pos * items_dev + lax.iota(jnp.int32, items_dev)[None, :]
    ).astype(jnp.float32)
    picked = jnp.dot(onehot, items, precision=high, preferred_element_type=jnp.float32)
    cand_col = lax.psum(picked, "row")
    across = (((1,), (1,)), ((), ()))
    cand_row = spread(lax.dynamic_slice_in_dim(cand_col, offset, width_row, 1), "col", root)
    image_part = lax.dot_general(
        cand_col, tile, across, precision=high, preferred_element_type=jnp.float32
    )
    image_row = lax.psum(image_part, "col")
    quad = jnp.where(col_pos == 0, jnp.sum(cand_row * image_row, axis=1), jnp.float32(0.0))
    linear = jnp.where(
        row_pos == 0,
        jnp.dot(cand_col, theta, precision=high, preferred_element_type=jnp.float32),
        jnp.float32(0.0),
    )
    quad_all, linear_all = lax.psum((quad, linear), ("row", "col"))
    return (tile, linear_all + jnp.sqrt(quad_all / F))


def solution(mesh):
    return jax.shard_map(
        body,
        mesh=mesh,
        in_specs=(P("row", "col"), P(), P("col"), P("row", "col"), P(), P("col")),
        out_specs=(P("row", "col"), P()),
        check_vma=False,
    )
```

profile of v0, /device:TPU:1, one launch (start us, length us, event | category | flops | bytes accessed | tf_op | source)
XLA Modules:
  0.0 940.3 jit_solution(5957106584917055528)
XLA Ops:
  7.2 0.0 copy-start
  7.2 0.0 all-gather.2.cloned.1.call-start
  7.2 1.3 dynamic_slice.9
  8.5 0.6 iota_compare_fusion
  9.2 2.3 broadcast_select_fusion
  11.5 0.0 all-gather.2.cloned.1.call-update
  11.5 0.0 all-reduce.8.cloned.1.call-start
  11.6 0.0 copy-done
  11.6 4.5 fusion
  16.1 0.0 all-reduce.8.cloned.1.call-update
  16.1 0.0 all-reduce.6.cloned.1.call-start
  16.2 90.8 %all-gather.2.cloned.1.call-done = f32[2048,2048]{1,0:T(8,128)} async-done(((f32[128,2048]{1,0:T(8,128)}), f32[2048,2048]{1,0:T(8,128)}) %all-gather.2.cloned.1.call-update) | async-done | bytes 16777232 | tf_op jit(solution)/shard_map/all_gather | solution.py:27
  107.0 8.7 dynamic-slice_select_fusion
  115.7 0.0 copy-start.3
  115.7 0.0 all-reduce.6.cloned.1.call-update
  115.7 0.0 all-reduce.10.cloned.1.call-start
  115.8 122.9 %all-reduce.8.cloned.1.call-done = f32[512,2048]{1,0:T(8,128)} async-done(((f32[512,2048]{1,0:T(8,128)}), f32[512,2048]{1,0:T(8,128)}) %all-reduce.8.cloned.1.call-update) | async-done | bytes 4194320 | tf_op jit(solution)/shard_map/psum | solution.py:40
  238.7 3.2 dynamic-slice_select_fusion.1
  241.9 343.4 %all-reduce.6.cloned.1.call-done = f32[2048,1024]{1,0:T(8,128)} async-done(((f32[2048,1024]{1,0:T(8,128)}), f32[2048,1024]{1,0:T(8,128)}) %all-reduce.6.cloned.1.call-update) | async-done | bytes 8388624 | tf_op jit(solution)/shard_map/psum | solution.py:12
  585.3 0.0 copy-done.3
  585.3 67.7 %select_add_fusion = f32[1024,2048]{1,0:T(8,128)S(1)} fusion(f32[2048]{0:T(1024)S(1)} %copy-done.3, s32[2048]{0:T(1024)S(1)} %iota_add_fusion, s32[1024]{0:T(1024)S(1)} %iota_add_fusion.1, f32[2048,1024]{1,0:T(8,128)} %all-reduce.6.cloned.1.call-done, f32[2048,2048]{1,0:T(8,128)} %all-gather.2.cloned.1.call-done), kind=kOutput, calls=%fused_computation | convolution fusion | flops 51545899008 | bytes 33574912 | tf_op jit(solution)/shard_map/dot_general | solution.py:29
  653.1 0.0 copy-start.4
  653.1 3.4 copy-done.4
  656.5 0.0 copy-done.1
  656.5 15.2 %fusion.5 = f32[512,1024]{1,0:T(8,128)} fusion(f32[512,2048]{1,0:T(8,128)S(1)} %copy-done.1, f32[1024,2048]{1,0:T(8,128)S(1)} %select_add_fusion), kind=kOutput, calls=%fused_computation.17 | convolution fusion | flops 12884901888 | bytes 14680064 | tf_op jit(solution)/shard_map/dot_general | solution.py:43
  671.7 0.0 all-reduce.10.cloned.1.call-update
  671.7 0.0 copy-done.2
  671.7 5.8 fusion.4
  677.5 185.2 %all-reduce.10.cloned.1.call-done = (f32[512,1024]{1,0:T(8,128)}, f32[512,1024]{1,0:T(8,128)}) async-done(((f32[512,1024]{1,0:T(8,128)}, f32[512,1024]{1,0:T(8,128)}), (f32[512,1024]{1,0:T(8,128)}, f32[512,1024]{1,0:T(8,128)})) %all-reduce.10.cloned.1.call-update) | async-done | bytes 4194320 | tf_op jit(solution)/shard_map/psum | solution.py:12
  862.7 2.5 multiply_reduce_fusion
  865.2 67.8 %all-reduce = (f32[512]{0:T(512)S(1)}, f32[512]{0:T(512)S(1)}) all-reduce(f32[512]{0:T(512)S(1)} %broadcast_select_fusion.2, f32[512]{0:T(512)S(1)} %broadcast_select_fusion.1), channel_id=1, replica_groups=mesh['row'=16,'col'=8] {'row','col'}, use_global_device_ids=true, to_apply=%region_2.3 | all-reduce | flops 1024 | bytes 8192 | tf_op jit(solution)/shard_map/psum | solution.py:53
  933.0 0.6 sqrt_add_fusion
  (7 shorter events, 0.0 us)
Async XLA Ops:
  7.2 4.4 copy-start
  7.2 99.8 %all-gather.2.cloned.1.call-start = ((), (), s32[]{:S(2)}) async-start(), calls=%async_computation | async-start | bytes 17825792 | tf_op jit(solution)/shard_map/all_gather | solution.py:27
  11.5 227.2 %all-reduce.8.cloned.1.call-start = ((), (), s32[]{:S(2)}) async-start(), calls=%async_computation.2 | async-start | bytes 8388608 | tf_op jit(solution)/shard_map/psum | solution.py:40
  16.1 569.2 %all-reduce.6.cloned.1.call-start = ((), (), s32[]{:S(2)}) async-start(), calls=%async_computation.1 | async-start | bytes 16777216 | tf_op jit(solution)/shard_map/psum | solution.py:12
  115.7 469.7 %copy-start.3 = (f32[2048]{0:T(1024)S(1)}, f32[2048]{0:T(1024)}, u32[]{:S(2)}) copy-start(f32[2048]{0:T(1024)} %param.8) | copy-start | bytes 24580
  115.7 747.0 %all-reduce.10.cloned.1.call-start = ((), (), s32[]{:S(2)}) async-start(), calls=%async_computation.3 | async-start | bytes 8388608 | tf_op jit(solution)/shard_map/psum | solution.py:12
  585.3 71.1 %copy-start.1 = (f32[512,2048]{1,0:T(8,128)S(1)}, f32[512,2048]{1,0:T(8,128)}, u32[]{:S(2)}) copy-start(f32[512,2048]{1,0:T(8,128)} %all-reduce.8.cloned.1.call-done) | copy-start | bytes 12582916
  653.1 3.4 copy-start.4
  656.5 15.3 %copy-start.2 = (f32[2048]{0:T(1024)S(1)}, f32[2048]{0:T(1024)}, u32[]{:S(2)}) copy-start(f32[2048]{0:T(1024)} %param.11) | copy-start | bytes 24580
Sparse Core Ops, SparseCore 0:
  11.7 95.2 all-gather.1
  109.5 129.1 all-reduce.7
  241.8 343.4 all-reduce.5
  671.8 190.8 all-reduce.9
where the time goes:
time: 944 us; the launch traced here: 940 us
  waiting for transfers between devices  742 us (79%)
  matrix products  93.2 us (10%)
  blocking collectives  67.8 us (7%)
  other arithmetic  18 us (2%)
  between operations  14.1 us (1%)
    psum x2, waiting for transfers between devices, spread(): return lax.psum(kept, axis)  529 us
    psum x1, waiting for transfers between devices, body(): cand_col = lax.psum(picked, 'row')  123 us
    all_gather x1, waiting for transfers between devices, body(): col_all = lax.all_gather(masked, 'row', axis=0, tiled=True)  90.8 us
    psum x1, blocking collectives, body(): quad_all, linear_all = lax.psum((quad, linear), ('row', 'col'))  67.8 us
    dot_general x1, matrix products, body(): lax.dot_general(row_all, col_all, contract, precision=high, preferred_ele...  67.7 us
  transfers between devices with their start and end apart: 4, of which 4 were waited for; matrix products, arithmetic and copies ran while one was open for 2% of the time, Pallas kernels for 0%

commit v1 on v0

--- a/solution.py
+++ b/solution.py
@@ -24,7 +24,10 @@
     offset = row_pos % ratio * width_row
     root = row_pos // ratio
     contract = (((0,), (0,)), ((), ()))
-    col_all = lax.all_gather(masked, "row", axis=0, tiled=True)
+    n_dev = lax.axis_size("row")
+    blocks = jnp.stack([masked for _ in range(n_dev)])
+    blocks = lax.all_to_all(blocks, "row", split_axis=0, concat_axis=0)
+    col_all = jnp.concatenate(blocks, axis=0)
     row_all = spread(lax.dynamic_slice_in_dim(col_all, offset, width_row, 1), "col", root)
     tile = lax.dot_general(
         row_all, col_all, contract, precision=high, preferred_element_type=jnp.float32

time: 944 us -> 986 us (1.044)
  waiting for transfers between devices: 742 us -> 771 us
    all_to_all x0 -> x1, waiting for transfers between devices: none -> 246 us  [body(): blocks = lax.all_to_all(blocks, 'row', split_axis=0, concat_axis=0)]
    psum x1, waiting for transfers between devices: 123 us -> 0.02 us  [body(): cand_col = lax.psum(picked, 'row')]
    all_gather x1 -> x0, waiting for transfers between devices: 90.8 us -> none  [body(): col_all = lax.all_gather(masked, 'row', axis=0, tiled=True)]
  transfers between devices with their start and end apart: 4 -> 4, of which waited for: 4 -> 3; matrix products, arithmetic and copies ran while one was open for 2% -> 2% of each run, Pallas kernels for 0% -> 0%
where the time goes in v1:
time: 986 us; the launch traced here: 982 us
  waiting for transfers between devices  771 us (78%)
  matrix products  92.5 us (9%)
  blocking collectives  67.8 us (7%)
  other arithmetic  17 us (2%)
  between operations  14.1 us (1%)
  local copies, waits for them, and re-layouts  12.6 us (1%)
    psum x2, waiting for transfers between devices, spread(): return lax.psum(kept, axis)  525 us
    all_to_all x1, waiting for transfers between devices, body(): blocks = lax.all_to_all(blocks, 'row', split_axis=0, concat_axis=0)  246 us
    psum x1, blocking collectives, body(): quad_all, linear_all = lax.psum((quad, linear), ('row', 'col'))  67.8 us
    dot_general x1, matrix products, body(): lax.dot_general(row_all, col_all, contract, precision=high, preferred_ele...  67.7 us
  transfers between devices with their start and end apart: 4, of which 3 were waited for; matrix products, arithmetic and copies ran while one was open for 2% of the time, Pallas kernels for 0%

profile of v1, /device:TPU:1, one launch (start us, length us, event | category | flops | bytes accessed | tf_op | source)
XLA Modules:
  0.0 982.0 jit_solution(4010384806060926025)
XLA Ops:
  7.2 0.0 copy-start
  7.2 1.3 dynamic_slice.9
  8.5 0.6 iota_compare_fusion
  9.1 1.4 broadcast_select_fusion
  10.5 7.9 stack.2
  18.4 7.3 all-to-all-start
  25.7 0.0 all-reduce.8.cloned.1.call-start
  25.7 0.0 copy-done
  25.7 0.0 copy-done.4
  25.7 3.8 fusion
  29.6 0.0 all-reduce.8.cloned.1.call-update
  29.6 0.0 all-reduce.6.cloned.1.call-start
  29.7 245.6 %all-to-all-done = f32[16,128,2048]{2,1,0:T(8,128)} async-done(((f32[16,128,2048]{2,1,0:T(8,128)}), f32[16,128,2048]{2,1,0:T(8,128)}, u32[]{:S(2)}, u32[]{:S(2)}) %all-to-all-start) | async-done | bytes 16777248 | tf_op jit(solution)/shard_map/all_to_all | solution.py:29
  275.3 8.7 dynamic-slice_select_fusion
  283.9 0.0 all-reduce.6.cloned.1.call-update
  284.0 0.0 all-reduce.10.cloned.1.call-start
  284.0 0.0 all-reduce.8.cloned.1.call-done
  284.1 3.2 dynamic-slice_select_fusion.1
  287.3 339.7 %all-reduce.6.cloned.1.call-done = f32[2048,1024]{1,0:T(8,128)} async-done(((f32[2048,1024]{1,0:T(8,128)}), f32[2048,1024]{1,0:T(8,128)}) %all-reduce.6.cloned.1.call-update) | async-done | bytes 8388624 | tf_op jit(solution)/shard_map/psum | solution.py:12
  627.0 0.0 copy-done.5
  627.0 67.7 %select_add_fusion = f32[1024,2048]{1,0:T(8,128)S(1)} fusion(f32[2048]{0:T(1024)S(1)} %copy-done.5, s32[2048]{0:T(1024)S(1)} %iota_add_fusion, s32[1024]{0:T(1024)S(1)} %iota_add_fusion.1, f32[2048,1024]{1,0:T(8,128)} %all-reduce.6.cloned.1.call-done, f32[2048,2048]{1,0:T(8,128)} %bitcast.1), kind=kOutput, calls=%fused_computation | convolution fusion | flops 51545899008 | bytes 33574912 | tf_op jit(solution)/shard_map/dot_general | solution.py:32
  694.7 0.0 copy-start.6
  694.8 3.4 copy-done.6
  698.1 0.0 copy-done.2
  698.2 15.2 %fusion.5 = f32[512,1024]{1,0:T(8,128)} fusion(f32[512,2048]{1,0:T(8,128)S(1)} %copy-done.2, f32[1024,2048]{1,0:T(8,128)S(1)} %select_add_fusion), kind=kOutput, calls=%fused_computation.17 | convolution fusion | flops 12884901888 | bytes 14680064 | tf_op jit(solution)/shard_map/dot_general | solution.py:46
  713.4 0.0 all-reduce.10.cloned.1.call-update
  713.4 5.8 fusion.4
  719.2 185.2 %all-reduce.10.cloned.1.call-done = (f32[512,1024]{1,0:T(8,128)}, f32[512,1024]{1,0:T(8,128)}) async-done(((f32[512,1024]{1,0:T(8,128)}, f32[512,1024]{1,0:T(8,128)}), (f32[512,1024]{1,0:T(8,128)}, f32[512,1024]{1,0:T(8,128)})) %all-reduce.10.cloned.1.call-update) | async-done | bytes 4194320 | tf_op jit(solution)/shard_map/psum | solution.py:12
  904.3 2.5 multiply_reduce_fusion
  906.8 67.8 %all-reduce = (f32[512]{0:T(512)S(1)}, f32[512]{0:T(512)S(1)}) all-reduce(f32[512]{0:T(512)S(1)} %broadcast_select_fusion.2, f32[512]{0:T(512)S(1)} %broadcast_select_fusion.1), channel_id=1, replica_groups=mesh['row'=16,'col'=8] {'row','col'}, use_global_device_ids=true, to_apply=%region_2.3 | all-reduce | flops 1024 | bytes 8192 | tf_op jit(solution)/shard_map/psum | solution.py:56
  974.6 0.6 sqrt_add_fusion
  975.2 0.0 copy-done.1
  (11 shorter events, 0.0 us)
Async XLA Ops:
  7.2 18.6 %copy-start = (f32[64,2048]{1,0:T(8,128)S(1)}, f32[64,2048]{1,0:T(8,128)}, u32[]{:S(2)}) copy-start(f32[64,2048]{1,0:T(8,128)} %param.9) | copy-start | bytes 1572868
  18.4 7.4 copy-start.4
  18.4 256.9 %all-to-all-start = ((f32[16,128,2048]{2,1,0:T(8,128)}), f32[16,128,2048]{2,1,0:T(8,128)}, u32[]{:S(2)}, u32[]{:S(2)}) async-start(f32[16,128,2048]{2,1,0:T(8,128)} %stack.2), calls=%async_computation | async-start | bytes 33554432 | tf_op jit(solution)/shard_map/all_to_all | solution.py:29
  25.7 258.4 %all-reduce.8.cloned.1.call-start = ((), (), s32[]{:S(2)}) async-start(), calls=%async_computation.2 | async-start | bytes 8388608 | tf_op jit(solution)/shard_map/psum | solution.py:43
  29.6 597.4 %all-reduce.6.cloned.1.call-start = ((), (), s32[]{:S(2)}) async-start(), calls=%async_computation.1 | async-start | bytes 16777216 | tf_op jit(solution)/shard_map/psum | solution.py:12
  283.9 343.1 %copy-start.5 = (f32[2048]{0:T(1024)S(1)}, f32[2048]{0:T(1024)}, u32[]{:S(2)}) copy-start(f32[2048]{0:T(1024)} %param.8) | copy-start | bytes 24580
  284.0 620.4 %all-reduce.10.cloned.1.call-start = ((), (), s32[]{:S(2)}) async-start(), calls=%async_computation.3 | async-start | bytes 8388608 | tf_op jit(solution)/shard_map/psum | solution.py:12
  627.0 71.1 %copy-start.2 = (f32[512,2048]{1,0:T(8,128)S(1)}, f32[512,2048]{1,0:T(8,128)}, u32[]{:S(2)}) copy-start(f32[512,2048]{1,0:T(8,128)} %all-reduce.8.cloned.1.call-done) | copy-start | bytes 12582916
  694.7 3.4 copy-start.6
  698.2 15.2 %copy-start.3 = (f32[2048]{0:T(1024)S(1)}, f32[2048]{0:T(1024)}, u32[]{:S(2)}) copy-start(f32[2048]{0:T(1024)} %param.11) | copy-start | bytes 24580
  698.2 277.1 %copy-start.1 = (f32[64,2048]{1,0:T(8,128)S(1)}, f32[64,2048]{1,0:T(8,128)}, u32[]{:S(2)}) copy-start(f32[64,2048]{1,0:T(8,128)} %param.9) | copy-start | bytes 1572868
Sparse Core Ops, SparseCore 0:
  29.7 244.2 all-reduce.7
  284.1 342.8 all-reduce.5
  713.5 190.7 all-reduce.9
